TPU v7x, 128 devices: a whole 4x4x4 slice. The times are simulated.
128 devices in a mesh: wide: 16 (over z, y), col: 8 (over x, core).
Axes of the slice: x: 4, y: 4, z: 4, core: 2. Of those that a mesh axis runs over, the one named last changes fastest.
Arguments:
- z_root: float32 [512, 16384], P('col', 'wide'), may hold values from -6 to 6
- z_child: float32 [512, 2, 8192], P('col', None, 'wide'), may hold values from -6 to 6
- z_grand: float32 [512, 4, 4096], P('col', None, 'wide'), may hold values from -6 to 6
- inv_root: float32 [16384, 16384], P('wide', 'col'), as said below
- inv_child: float32 [2, 8192, 8192], P(None, 'wide', 'col'), as said below
- inv_grand: float32 [4, 4096, 4096], P(None, 'wide', 'col'), as said below
- panel_child: float32 [2, 4096, 8192], P(None, 'col', 'wide'), may hold values from -0.046875 to 0.046875
- panel_grand: float32 [4, 2048, 4096], P(None, 'col', 'wide'), may hold values from -0.0625 to 0.0625
- anc_child: int32 [2, 32], P(None, 'col'), may hold values from 0 to 127, as said below
- anc_grand: int32 [4, 16], P(None, 'col'), may hold values from 0 to 255, as said below
Outputs:
- x_root: float32 [512, 16384], P('wide', 'col')
- x_child: float32 [512, 2, 8192], P('wide', None, 'col')
- x_grand: float32 [512, 4, 4096], P('wide', None, 'col')
Inputs may be any that keep to these rules, and one draw needn't show every extreme that they name: inv_root is lower triangular with a positive diagonal (entries above the diagonal are zero). Each inv_child[k] is lower triangular with a positive diagonal. Each inv_grand[g] is lower triangular with a positive diagonal. `anc_child`: each row lists distinct blocks in rising order and always names block 0 and block 127. `anc_grand`: row g lists 2048 // 256 distinct root blocks in rising order, block 0 and block 127 among them, then as many distinct blocks of child g // 2 (numbered 16384 // 128 + (g // 2) * 64 onwards) in rising order, its first and its last among them.
All inputs are finite; a program needn't handle non-finite values.
Results may differ from a plain program's by a relative error of at most 0.000096.
Values sent between devices are 32-bit elements; how exact they have to be, the bound alone decides.
No kernel may reach another device: no remote copies, remote signals or barrier semaphores. Data moves between devices by JAX's collectives and lax.ppermute only.
A program may use at most 128 MiB of HBM per device.

v0:
```python
import jax
import jax.numpy as jnp
from jax import lax
from jax.sharding import PartitionSpec as P

BLK = 128
PRECISE = lax.Precision.HIGHEST


def pick_blocks(source_rows, blocks):
    leading = source_rows.shape[0]
    tiled = source_rows.reshape(leading, source_rows.shape[1] // BLK, BLK)
    selected = jnp.take(tiled, blocks.reshape(-1), axis=1)
    return selected.reshape(leading, blocks.shape[0], blocks.shape[1] * BLK)


def spread_rhs(local_part):
    return lax.all_gather(local_part, "col", axis=0, tiled=True)


def solve_terms(right_rows, inverse):
    return lax.psum_scatter(
        jnp.einsum(
            "ski,kij->skj",
            right_rows,
            inverse,
            precision=PRECISE,
            preferred_element_type=jnp.float32,
        ),
        "wide",
        scatter_dimension=0,
        tiled=True,
    )


def spread_solved(solved_local):
    gathered = lax.all_gather(solved_local, "col", axis=2, tiled=True)
    return gathered.reshape(gathered.shape[0], -1)


def fetch_ancestors(source_rows, blocks):
    return lax.all_gather(pick_blocks(source_rows, blocks), "wide", axis=0, tiled=True)


def finish_level(z_local, inverse, partial_value):
    summed = lax.psum(partial_value, "col")
    right_side = spread_rhs(z_local) - summed
    solved = solve_terms(right_side, inverse)
    return solved


def per_device(
    z_root,
    z_child,
    z_grand,
    inv_root,
    inv_child,
    inv_grand,
    panel_child,
    panel_grand,
    anc_child,
    anc_grand,
):
    root_right = spread_rhs(z_root[:, None, :])
    root_solved = solve_terms(root_right, inv_root[None])
    x_root = root_solved[:, 0, :]
    root_rows = spread_solved(root_solved)
    near_rows = fetch_ancestors(root_rows, anc_child)
    partial_value = jnp.einsum(
        "ska,kaj->skj",
        near_rows,
        panel_child,
        precision=PRECISE,
        preferred_element_type=jnp.float32,
    )
    x_child = finish_level(z_child, inv_child, partial_value)
    child_rows = spread_solved(x_child)
    solved_all = jnp.concatenate([root_rows, child_rows], axis=1)
    far_rows = fetch_ancestors(solved_all, anc_grand)
    partial_grand = jnp.einsum(
        "sga,gaj->sgj", far_rows, panel_grand, precision=PRECISE, preferred_element_type=jnp.float32
    )
    x_grand = finish_level(z_grand, inv_grand, partial_grand)
    return (x_root, x_child, x_grand)


def solution(mesh):
    in_specs = (
        P("col", "wide"),
        P("col", None, "wide"),
        P("col", None, "wide"),
        P("wide", "col"),
        P(None, "wide", "col"),
        P(None, "wide", "col"),
        P(None, "col", "wide"),
        P(None, "col", "wide"),
        P(None, "col"),
        P(None, "col"),
    )
    out_specs = (P("wide", "col"), P("wide", None, "col"), P("wide", None, "col"))
    return jax.shard_map(
        per_device, mesh=mesh, in_specs=in_specs, out_specs=out_specs, check_vma=False
    )
```

profile of v0, /device:TPU:0, one launch (start us, length us, event | category | flops | bytes accessed | tf_op | source)
XLA Modules:
  0.0 726.2 jit_solution(2255232434404925078)
XLA Ops:
  7.2 0.0 all-gather.21.cloned.1.call-start
  7.2 0.7 all-gather.21.cloned.1.call-update
  7.9 0.0 all-reduce.9.cloned.1.call-start
  8.0 29.4 %all-gather.21.cloned.1.call-done = f32[512,1024]{1,0:T(8,128)} async-done(((f32[64,1024]{1,0:T(8,128)}), f32[512,1024]{1,0:T(8,128)}) %all-gather.21.cloned.1.call-update) | async-done | bytes 2097168 | tf_op jit(solution)/shard_map/all_gather | solution.py:18
  37.4 30.4 %convolution_bitcast_fusion = f32[512,1,2048]{0,2,1:T(8,128)} fusion(f32[1024,2048]{1,0:T(8,128)} %param.13, f32[512,1024]{1,0:T(8,128)} %all-gather.21.cloned.1.call-done), kind=kOutput, calls=%fused_computation.3 | convolution fusion | flops 12884901888 | bytes 14680064 | tf_op jit(solution)/shard_map/ski,kij->skj/dot_general | solution.py:23
  67.8 11.0 %copy.75 = f32[512,1,2048]{2,1,0:T(1,128)} copy(f32[512,1,2048]{0,2,1:T(8,128)} %convolution_bitcast_fusion) | data formatting | bytes 8388608 | tf_op jit(solution)/shard_map/ski,kij->skj/transpose | solution.py:23
  78.8 0.0 all-reduce.9.cloned.1.call-update
  78.8 0.0 all-gather.11.cloned.1.call-start
  78.9 0.6 copy-done.8
  79.5 0.6 dynamic-slice
  80.7 102.2 %all-reduce.9.cloned.1.call-done = f32[512,1,2048]{2,1,0:T(1,128)} async-done(((f32[512,1,2048]{2,1,0:T(1,128)}), f32[512,1,2048]{2,1,0:T(1,128)}) %all-reduce.9.cloned.1.call-update) | async-done | bytes 4194320
  183.0 1.7 constant_dynamic-slice_fusion
  184.6 0.0 all-gather.11.cloned.1.call-update
  184.7 0.0 all-gather.13.cloned.1.call-start
  184.7 0.1 reshape.104
  184.8 0.1 broadcast_bitcast_fusion.1
  184.9 25.1 %all-gather.11.cloned.1.call-done = f32[32,1,16384]{2,1,0:T(1,128)} async-done(((f32[32,1,2048]{2,1,0:T(1,128)}), f32[32,1,16384]{2,1,0:T(1,128)}) %all-gather.11.cloned.1.call-update) | async-done | bytes 2097168 | tf_op jit(solution)/shard_map/all_gather | solution.py:37
  210.0 4.2 copy.77
  214.3 2.1 gather_fusion
  216.4 0.1 copy.78
  216.5 0.1 gather.13
  216.6 0.7 copy_select_fusion.1
  217.3 0.0 all-gather.13.cloned.1.call-update
  217.3 0.0 all-gather.9.cloned.1.call-start
  217.3 0.8 copy.76
  218.1 0.0 all-gather.9.cloned.1.call-update
  218.1 0.0 all-reduce.5.cloned.1.call-start
  218.2 44.9 %all-gather.13.cloned.1.call-done = f32[512,2,512]{2,0,1:T(8,128)} async-done(((f32[32,2,512]{2,0,1:T(8,128)}), f32[512,2,512]{2,0,1:T(8,128)}) %all-gather.13.cloned.1.call-update) | async-done | bytes 2097168 | tf_op jit(solution)/shard_map/all_gather | solution.py:42
  263.0 7.0 convolution_bitcast_fusion.4
  270.1 0.0 all-reduce.5.cloned.1.call-update
  270.1 0.0 reduce-scatter.3.cloned.1.call-start
  270.1 19.4 %all-gather.9.cloned.1.call-done = f32[512,2,512]{2,0,1:T(8,128)} async-done(((f32[64,2,512]{2,0,1:T(8,128)}), f32[512,2,512]{2,0,1:T(8,128)}) %all-gather.9.cloned.1.call-update) | async-done | bytes 2097168 | tf_op jit(solution)/shard_map/all_gather | solution.py:18
  289.6 68.2 %all-reduce.5.cloned.1.call-done = f32[512,2,512]{2,0,1:T(8,128)} async-done(((f32[512,2,512]{2,0,1:T(8,128)}), f32[512,2,512]{2,0,1:T(8,128)}) %all-reduce.5.cloned.1.call-update) | async-done | bytes 2097168 | tf_op jit(solution)/shard_map/psum | solution.py:46
  357.8 12.2 %convolution_bitcast_fusion.2 = f32[512,2,1024]{2,0,1:T(8,128)} fusion(f32[2,512,1024]{2,1,0:T(8,128)} %param.14, f32[512,2,512]{2,0,1:T(8,128)} %all-gather.9.cloned.1.call-done, f32[512,2,512]{2,0,1:T(8,128)} %all-reduce.5.cloned.1.call-done), kind=kOutput, calls=%fused_computation.5 | convolution fusion | flops 6442975232 | bytes 12582912 | tf_op jit(solution)/shard_map/ski,kij->skj/dot_general | solution.py:23
  370.0 0.0 reduce-scatter.3.cloned.1.call-update
  370.0 0.0 all-gather.17.cloned.1.call-start
  370.1 77.5 %reduce-scatter.3.cloned.1.call-done = f32[32,2,1024]{2,0,1:T(8,128)} async-done(((f32[512,2,1024]{2,0,1:T(8,128)}), f32[32,2,1024]{2,0,1:T(8,128)}) %reduce-scatter.3.cloned.1.call-update) | async-done | bytes 262160 | tf_op jit(solution)/shard_map/reduce_scatter | solution.py:22
  447.6 0.0 all-gather.19.cloned.1.call-start
  447.6 0.1 copy.84
  447.7 0.1 reshape.105
  447.9 0.1 broadcast_bitcast_fusion
  447.9 25.8 %all-gather.17.cloned.1.call-done = f32[32,2,8192]{2,0,1:T(8,128)} async-done(((f32[32,2,1024]{2,0,1:T(8,128)}), f32[32,2,8192]{2,0,1:T(8,128)}) %all-gather.17.cloned.1.call-update) | async-done | bytes 2097168 | tf_op jit(solution)/shard_map/all_gather | solution.py:37
  473.7 4.6 copy.81
  478.3 4.0 concatenate.6
  482.3 3.0 copy.83
  485.3 2.4 pad_maximum_fusion
  487.7 2.8 gather_fusion.1
  490.5 0.1 copy.85
  490.6 0.1 gather.15
  490.7 0.7 copy_select_fusion
  491.4 0.0 all-gather.15.cloned.1.call-start
  491.4 1.7 copy.80
  493.2 0.0 all-reduce.7.cloned.1.call-start
  493.2 43.9 %all-gather.19.cloned.1.call-done = f32[512,4,256]{2,0,1:T(8,128)} async-done(((f32[32,4,256]{2,0,1:T(8,128)}), f32[512,4,256]{2,0,1:T(8,128)}) %all-gather.19.cloned.1.call-update) | async-done | bytes 2097168 | tf_op jit(solution)/shard_map/all_gather | solution.py:42
  537.1 4.9 convolution_bitcast_fusion.3
  542.0 0.0 reduce-scatter.5.cloned.1.call-start
  542.1 21.7 %all-gather.15.cloned.1.call-done = f32[512,4,256]{2,0,1:T(8,128)} async-done(((f32[64,4,256]{2,0,1:T(8,128)}), f32[512,4,256]{2,0,1:T(8,128)}) %all-gather.15.cloned.1.call-update) | async-done | bytes 2097168 | tf_op jit(solution)/shard_map/all_gather | solution.py:18
  563.8 68.5 %all-reduce.7.cloned.1.call-done = f32[512,4,256]{2,0,1:T(8,128)} async-done(((f32[512,4,256]{2,0,1:T(8,128)}), f32[512,4,256]{2,0,1:T(8,128)}) %all-reduce.7.cloned.1.call-update) | async-done | bytes 2097168 | tf_op jit(solution)/shard_map/psum | solution.py:46
  632.3 7.8 %convolution_bitcast_fusion.1 = f32[512,4,512]{2,0,1:T(8,128)} fusion(f32[4,256,512]{2,1,0:T(8,128)S(1)} %copy-done, f32[512,4,256]{2,0,1:T(8,128)} %all-gather.15.cloned.1.call-done, f32[512,4,256]{2,0,1:T(8,128)} %all-reduce.7.cloned.1.call-done), kind=kOutput, calls=%fused_computation.4 | convolution fusion | flops 3221749760 | bytes 10485760 | tf_op jit(solution)/shard_map/ski,kij->skj/dot_general | solution.py:23
  640.0 0.9 copy-done.2
  641.0 0.8 copy.95
  641.8 0.9 copy.87
  642.7 74.9 %reduce-scatter.5.cloned.1.call-done = f32[32,4,512]{2,0,1:T(8,128)} async-done(((f32[512,4,512]{2,0,1:T(8,128)}), f32[32,4,512]{2,0,1:T(8,128)}) %reduce-scatter.5.cloned.1.call-update) | async-done | bytes 262160 | tf_op jit(solution)/shard_map/reduce_scatter | solution.py:22
  717.6 1.8 copy.88
  (28 shorter events, 0.2 us)
Async XLA Ops:
  7.2 625.1 %copy-start = (f32[4,256,512]{2,1,0:T(8,128)S(1)}, f32[4,256,512]{2,1,0:T(8,128)}, u32[]{:S(2)}) copy-start(f32[4,256,512]{2,1,0:T(8,128)} %param.15) | copy-start | bytes 6291460
  7.2 30.2 %all-gather.21.cloned.1.call-start = ((), (), s32[]{:S(2)}) async-start(), calls=%async_computation.12 | async-start | bytes 2359296 | tf_op jit(solution)/shard_map/all_gather | solution.py:18
  7.9 175.0 %all-reduce.9.cloned.1.call-start = ((), (), s32[]{:S(2)}) async-start(), calls=%async_computation.13 | async-start | bytes 8388608
  78.8 0.7 copy-start.8
  78.8 105.9 %copy-start.7 = (s32[2,4]{1,0:T(2,128)S(1)}, s32[2,4]{1,0:T(2,128)}, u32[]{:S(2)}) copy-start(s32[2,4]{1,0:T(2,128)} %param.18) | copy-start | bytes 100
  78.8 131.2 %all-gather.11.cloned.1.call-start = ((), (), s32[]{:S(2)}) async-start(), calls=%async_computation.3 | async-start | bytes 2359296 | tf_op jit(solution)/shard_map/all_gather | solution.py:37
  184.7 78.4 %all-gather.13.cloned.1.call-start = ((), (), s32[]{:S(2)}) async-start(), calls=%async_computation.4 | async-start | bytes 2228224 | tf_op jit(solution)/shard_map/all_gather | solution.py:42
  210.0 7.3 %copy-start.5 = (f32[64,2,512]{2,1,0:T(2,128)S(1)}, f32[64,2,512]{2,1,0:T(2,128)}, u32[]{:S(2)}) copy-start(f32[64,2,512]{2,1,0:T(2,128)} %param.11) | copy-start | bytes 786436
  217.3 72.3 %all-gather.9.cloned.1.call-start = ((), (), s32[]{:S(2)}) async-start(), calls=%async_computation.2 | async-start | bytes 2359296 | tf_op jit(solution)/shard_map/all_gather | solution.py:18
  218.1 139.7 %all-reduce.5.cloned.1.call-start = ((), (), s32[]{:S(2)}) async-start(), calls=%async_computation.5 | async-start | bytes 4194304 | tf_op jit(solution)/shard_map/psum | solution.py:46
  270.1 177.5 %reduce-scatter.3.cloned.1.call-start = ((), (), s32[]{:S(2)}) async-start(), calls=%async_computation.6 | async-start | bytes 4456448 | tf_op jit(solution)/shard_map/reduce_scatter | solution.py:22
  370.0 77.7 %copy-start.6 = (s32[4,2]{0,1:T(2,128)S(1)}, s32[4,2]{0,1:T(2,128)}, u32[]{:S(2)}) copy-start(s32[4,2]{0,1:T(2,128)} %param.19) | copy-start | bytes 100
  370.0 103.7 %all-gather.17.cloned.1.call-start = ((), (), s32[]{:S(2)}) async-start(), calls=%async_computation.8 | async-start | bytes 2359296 | tf_op jit(solution)/shard_map/all_gather | solution.py:37
  447.6 89.6 %all-gather.19.cloned.1.call-start = ((), (), s32[]{:S(2)}) async-start(), calls=%async_computation.9 | async-start | bytes 2228224 | tf_op jit(solution)/shard_map/all_gather | solution.py:42
  482.3 3.0 copy-start.1
  487.7 49.5 %copy-start.3 = (f32[4,256,256]{2,1,0:T(8,128)S(1)}, f32[4,256,256]{2,1,0:T(8,128)}, u32[]{:S(2)}) copy-start(f32[4,256,256]{2,1,0:T(8,128)} %param.17) | copy-start | bytes 3145732
  491.4 72.4 %all-gather.15.cloned.1.call-start = ((), (), s32[]{:S(2)}) async-start(), calls=%async_computation.7 | async-start | bytes 2359296 | tf_op jit(solution)/shard_map/all_gather | solution.py:18
  493.2 139.1 %all-reduce.7.cloned.1.call-start = ((), (), s32[]{:S(2)}) async-start(), calls=%async_computation.10 | async-start | bytes 4194304 | tf_op jit(solution)/shard_map/psum | solution.py:46
  542.0 175.5 %reduce-scatter.5.cloned.1.call-start = ((), (), s32[]{:S(2)}) async-start(), calls=%async_computation.11 | async-start | bytes 4456448 | tf_op jit(solution)/shard_map/reduce_scatter | solution.py:22
  640.0 0.9 copy-start.2
  640.0 1.7 copy-start.4
Sparse Core Ops, SparseCore 0:
  9.7 27.5 all-gather.20
  79.0 103.9 all-reduce.8
  185.2 24.7 all-gather.10
  217.4 45.5 all-gather.12
  265.2 24.3 all-gather.8
  291.8 65.9 all-reduce.4
  370.1 77.3 reduce-scatter.2
  449.4 24.3 all-gather.16
  491.5 45.5 all-gather.18
  539.4 24.3 all-gather.14
  566.3 65.9 all-reduce.6
  640.2 77.3 reduce-scatter.4
where the time goes:
time: 727 us; the launch traced here: 726 us
  waiting for transfers between devices  602 us (83%)
  matrix products  62.3 us (9%)
  local copies, waits for them, and re-layouts  42.2 us (6%)
  between operations  15 us (2%)
    reduce_scatter x2, waiting for transfers between devices, solve_terms(): lax.psum_scatter(jnp.einsum('ski,kij->skj', right_rows, inverse, precisio...  152 us
    psum x2, waiting for transfers between devices, finish_level(): summed = lax.psum(partial_value, 'col')  137 us
    unnamed x13, waiting for transfers between devices  103 us
    all_gather x2, waiting for transfers between devices, fetch_ancestors(): lax.all_gather(pick_blocks(source_rows, blocks), 'wide', axis=0, tiled=True)  88.8 us
    all_gather x3, waiting for transfers between devices, spread_rhs(): return lax.all_gather(local_part, 'col', axis=0, tiled=True)  70.5 us
    all_gather x2, waiting for transfers between devices, spread_solved(): gathered = lax.all_gather(solved_local, 'col', axis=2, tiled=True)  50.9 us
    dot_general x3, matrix products, solve_terms(): jnp.einsum('ski,kij->skj', right_rows, inverse, precision=PRECISE, prefer...  50.4 us
  transfers between devices with their start and end apart: 12, of which 12 were waited for; matrix products, arithmetic and copies ran while one was open for 2% of the time, Pallas kernels for 0%

commit v1 on v0

--- a/solution.py
+++ b/solution.py
@@ -1,3 +1,4 @@
+import functools
 import jax
 import jax.numpy as jnp
 from jax import lax
@@ -5,6 +6,33 @@
 
 BLK = 128
 PRECISE = lax.Precision.HIGHEST
+
+
+def _proceed_sides(in_array, array_dim):
+    answer = lax.axis_size("col")
+    block_now = lax.axis_index("col")
+    r_now, arr_out, y2 = (answer, block_now, in_array.shape[array_dim])
+    nodes = [b * r_now if num == array_dim else b for num, b in enumerate(in_array.shape)]
+    spare = jnp.zeros(nodes, in_array.dtype)
+    shaped = lax.dynamic_update_slice_in_dim(spare, in_array, arr_out * y2, axis=array_dim)
+    carry_out = earlier = in_array
+    for q in range(1, r_now // 2 + 1):
+        k_now = list(map(lambda num: (num, (num + 1) % r_now), range(r_now)))
+        carry_out = lax.ppermute(carry_out, axis_name="col", perm=k_now)
+        shaped = lax.dynamic_update_slice_in_dim(
+            shaped, carry_out, (arr_out - q) % r_now * y2, axis=array_dim
+        )
+        if 2 * q < r_now:
+            current_value = range(r_now)
+            s_next = map(lambda num: (num, (num - 1) % r_now), current_value)
+            earlier = lax.ppermute(earlier, axis_name="col", perm=list(s_next))
+            shaped = lax.dynamic_update_slice_in_dim(
+                shaped, earlier, (arr_out + q) % r_now * y2, axis=array_dim
+            )
+    return shaped
+
+
+_replace_table = functools.partial(_proceed_sides, array_dim=0)
 
 
 def pick_blocks(source_rows, blocks):
@@ -15,7 +43,7 @@
 
 
 def spread_rhs(local_part):
-    return lax.all_gather(local_part, "col", axis=0, tiled=True)
+    return _replace_table(local_part)
 
 
 def solve_terms(right_rows, inverse):

time: 727 us -> 630 us (0.87)
  waiting for transfers between devices: 602 us -> 495 us
  starting transfers between devices: 0.49 us -> 23.9 us
  matrix products: 62.3 us -> 49.4 us
    unnamed x13 -> x9, waiting for transfers between devices: 103 us -> 0.15 us
    reduce_scatter x2 -> x3, waiting for transfers between devices: 152 us -> 231 us  [solve_terms(): lax.psum_scatter(jnp.einsum('ski,kij->skj', right_rows, inverse, precisio...]
    all_gather x3 -> x0, waiting for transfers between devices: 70.5 us -> none  [spread_rhs(): return lax.all_gather(local_part, 'col', axis=0, tiled=True)]
    ppermute x0 -> x21, waiting for transfers between devices: none -> 41.9 us  [the longest x12 35.2 us: _proceed_sides(): carry_out = lax.ppermute(carry_out, axis_name='col', perm=k_now)]
    psum x2, waiting for transfers between devices: 137 us -> 98.2 us  [finish_level(): summed = lax.psum(partial_value, 'col')]
    ppermute x0 -> x21, starting transfers between devices: none -> 23.1 us  [the longest x9 22.6 us: _proceed_sides(): earlier = lax.ppermute(earlier, axis_name='col', perm=list(s_next))]
    all_gather x2, waiting for transfers between devices: 88.8 us -> 72.1 us  [fetch_ancestors(): lax.all_gather(pick_blocks(source_rows, blocks), 'wide', axis=0, tiled=True)]
    dot_general x3, matrix products: 50.4 us -> 37.4 us  [solve_terms(): jnp.einsum('ski,kij->skj', right_rows, inverse, precision=PRECISE, prefer...]
  transfers between devices with their start and end apart: 12 -> 30, of which waited for: 12 -> 21; matrix products, arithmetic and copies ran while one was open for 2% -> 5% of each run, Pallas kernels for 0% -> 0%
where the time goes in v1:
time: 630 us; the launch traced here: 629 us
  waiting for transfers between devices  495 us (79%)
  matrix products  49.4 us (8%)
  local copies, waits for them, and re-layouts  42.8 us (7%)
  starting transfers between devices  23.9 us (4%)
  between operations  14.1 us (2%)
    reduce_scatter x3, waiting for transfers between devices, solve_terms(): lax.psum_scatter(jnp.einsum('ski,kij->skj', right_rows, inverse, precisio...  231 us
    psum x2, waiting for transfers between devices, finish_level(): summed = lax.psum(partial_value, 'col')  98.2 us
    all_gather x2, waiting for transfers between devices, fetch_ancestors(): lax.all_gather(pick_blocks(source_rows, blocks), 'wide', axis=0, tiled=True)  72.1 us
    all_gather x2, waiting for transfers between devices, spread_solved(): gathered = lax.all_gather(solved_local, 'col', axis=2, tiled=True)  51.8 us
    dot_general x3, matrix products, solve_terms(): jnp.einsum('ski,kij->skj', right_rows, inverse, precision=PRECISE, prefer...  37.4 us
    ppermute x12, waiting for transfers between devices, _proceed_sides(): carry_out = lax.ppermute(carry_out, axis_name='col', perm=k_now)  35.2 us
    ppermute x9, starting transfers between devices, _proceed_sides(): earlier = lax.ppermute(earlier, axis_name='col', perm=list(s_next))  22.6 us
  transfers between devices with their start and end apart: 30, of which 21 were waited for; matrix products, arithmetic and copies ran while one was open for 5% of the time, Pallas kernels for 0%

profile of v1, /device:TPU:0, one launch (start us, length us, event | category | flops | bytes accessed | tf_op | source)
XLA Modules:
  0.0 629.2 jit_solution(11453861854139410501)
XLA Ops:
  7.3 2.9 collective-permute-start.1
  10.5 4.0 collective-permute-done
  14.5 3.0 collective-permute-start.3
  17.5 4.0 collective-permute-done.2
  21.5 3.0 collective-permute-start.5
  24.5 4.0 collective-permute-done.4
  28.6 6.9 %collective-permute-done.6 = f32[64,1,1024]{2,0,1:T(8,128)S(1)} collective-permute-done((f32[64,1,1024]{2,0,1:T(8,128)S(1)}, f32[64,1,1024]{2,0,1:T(8,128)S(1)}, u32[]{:S(2)}, u32[]{:S(2)}) %collective-permute-start.6) | collective-permute-done | bytes 262176 | tf_op jit(solution)/shard_map/ppermute | solution.py:21
  35.5 17.4 %convolution_bitcast_fusion = f32[512,1,2048]{2,0,1:T(8,128)} fusion(f32[512,1024]{1,0:T(8,128)S(1)} %bitcast_dynamic-update-slice_fusion, f32[1024,2048]{1,0:T(8,128)} %param.13), kind=kOutput, calls=%fused_computation.3 | convolution fusion | flops 12884901888 | bytes 14680064 | tf_op jit(solution)/shard_map/ski,kij->skj/dot_general | solution.py:51
  53.0 77.9 %reduce-scatter.4.cloned.1.call-done = f32[32,1,2048]{2,0,1:T(8,128)} async-done(((f32[512,1,2048]{2,0,1:T(8,128)}), f32[32,1,2048]{2,0,1:T(8,128)}) %reduce-scatter.4.cloned.1.call-update) | async-done | bytes 262160 | tf_op jit(solution)/shard_map/reduce_scatter | solution.py:50
  131.3 26.3 %all-gather.5.cloned.1.call-done = f32[32,1,16384]{2,0,1:T(8,128)} async-done(((f32[32,1,2048]{2,0,1:T(8,128)}), f32[32,1,16384]{2,0,1:T(8,128)}) %all-gather.5.cloned.1.call-update) | async-done | bytes 2097168 | tf_op jit(solution)/shard_map/all_gather | solution.py:65
  157.7 2.0 copy.74
  159.6 2.6 copy.59
  162.2 2.2 gather_fusion
  165.5 1.6 broadcast_in_dim.40
  167.1 0.8 fusion.5
  168.2 2.7 collective-permute-start.8
  170.9 4.1 collective-permute-done.7
  174.9 36.1 %all-gather.7.cloned.1.call-done = f32[512,2,512]{2,0,1:T(8,128)} async-done(((f32[32,2,512]{2,0,1:T(8,128)}), f32[512,2,512]{2,0,1:T(8,128)}) %all-gather.7.cloned.1.call-update) | async-done | bytes 2097168 | tf_op jit(solution)/shard_map/all_gather | solution.py:70
  211.1 7.1 %convolution_bitcast_fusion.4 = f32[512,2,512]{2,0,1:T(8,128)} fusion(f32[512,2,512]{2,0,1:T(8,128)} %all-gather.7.cloned.1.call-done, f32[2,512,512]{2,1,0:T(8,128)} %param.16), kind=kOutput, calls=%fused_computation.9 | convolution fusion | flops 3221225472 | bytes 6291456 | tf_op jit(solution)/shard_map/ska,kaj->skj/dot_general | solution.py:97
  218.2 1.1 collective-permute-start.10
  219.3 0.7 constant_dynamic-update-slice_fusion.14
  220.1 0.7 constant_dynamic-update-slice_fusion.13
  220.8 2.4 collective-permute-done.10
  223.2 3.1 collective-permute-start.12
  226.3 0.7 constant_dynamic-update-slice_fusion.12
  227.0 0.7 constant_dynamic-update-slice_fusion.11
  227.8 0.7 constant_dynamic-update-slice_fusion.10
  228.5 1.7 collective-permute-done.12
  230.2 0.7 constant_dynamic-update-slice_fusion.9
  230.9 4.1 collective-permute-done.13
  235.0 0.7 constant_dynamic-update-slice_fusion.8
  235.7 49.0 %all-reduce.3.cloned.1.call-done = f32[512,2,512]{2,0,1:T(8,128)} async-done(((f32[512,2,512]{2,0,1:T(8,128)}), f32[512,2,512]{2,0,1:T(8,128)}) %all-reduce.3.cloned.1.call-update) | async-done | bytes 2097168 | tf_op jit(solution)/shard_map/psum | solution.py:74
  284.8 12.2 %convolution_bitcast_fusion.2 = f32[512,2,1024]{2,0,1:T(8,128)} fusion(f32[2,512,1024]{2,1,0:T(8,128)} %param.14, f32[512,2,512]{2,0,1:T(8,128)} %constant_dynamic-update-slice_fusion.8, f32[512,2,512]{2,0,1:T(8,128)} %all-reduce.3.cloned.1.call-done), kind=kOutput, calls=%fused_computation.5 | convolution fusion | flops 6442975232 | bytes 12582912 | tf_op jit(solution)/shard_map/ski,kij->skj/dot_general | solution.py:51
  297.1 77.5 %reduce-scatter.6.cloned.1.call-done = f32[32,2,1024]{2,0,1:T(8,128)} async-done(((f32[512,2,1024]{2,0,1:T(8,128)}), f32[32,2,1024]{2,0,1:T(8,128)}) %reduce-scatter.6.cloned.1.call-update) | async-done | bytes 262160 | tf_op jit(solution)/shard_map/reduce_scatter | solution.py:50
  374.9 25.5 %all-gather.9.cloned.1.call-done = f32[32,2,8192]{2,0,1:T(8,128)} async-done(((f32[32,2,1024]{2,0,1:T(8,128)}), f32[32,2,8192]{2,0,1:T(8,128)}) %all-gather.9.cloned.1.call-update) | async-done | bytes 2097168 | tf_op jit(solution)/shard_map/all_gather | solution.py:65
  400.4 4.6 copy.65
  405.0 4.0 concatenate.6
  409.0 3.0 copy.67
  412.0 2.4 pad_maximum_fusion
  414.4 2.8 gather_fusion.1
  418.2 1.6 broadcast_in_dim.45
  419.8 0.9 fusion.4
  420.9 2.7 collective-permute-start.15
  423.6 4.4 collective-permute-done.14
  427.9 36.0 %all-gather.11.cloned.1.call-done = f32[512,4,256]{2,0,1:T(8,128)} async-done(((f32[32,4,256]{2,0,1:T(8,128)}), f32[512,4,256]{2,0,1:T(8,128)}) %all-gather.11.cloned.1.call-update) | async-done | bytes 2097168 | tf_op jit(solution)/shard_map/all_gather | solution.py:70
  463.9 4.9 convolution_bitcast_fusion.3
  468.9 1.1 collective-permute-start.17
  470.0 1.7 constant_dynamic-update-slice_fusion.6
  471.7 1.7 constant_dynamic-update-slice_fusion.5
  473.3 0.9 collective-permute-done.17
  474.2 3.0 collective-permute-start.19
  477.2 0.7 constant_dynamic-update-slice_fusion.4
  477.9 0.7 constant_dynamic-update-slice_fusion.3
  478.7 0.7 constant_dynamic-update-slice_fusion.2
  479.4 1.7 collective-permute-done.19
  481.1 0.7 constant_dynamic-update-slice_fusion.1
  481.8 3.8 collective-permute-done.20
  485.6 0.7 constant_dynamic-update-slice_fusion
  486.4 49.1 %all-reduce.5.cloned.1.call-done = f32[512,4,256]{2,0,1:T(8,128)} async-done(((f32[512,4,256]{2,0,1:T(8,128)}), f32[512,4,256]{2,0,1:T(8,128)}) %all-reduce.5.cloned.1.call-update) | async-done | bytes 2097168 | tf_op jit(solution)/shard_map/psum | solution.py:74
  535.5 7.8 %convolution_bitcast_fusion.1 = f32[512,4,512]{2,0,1:T(8,128)} fusion(f32[4,256,512]{2,1,0:T(8,128)S(1)} %copy-done, f32[512,4,256]{2,0,1:T(8,128)} %constant_dynamic-update-slice_fusion, f32[512,4,256]{2,0,1:T(8,128)} %all-reduce.5.cloned.1.call-done), kind=kOutput, calls=%fused_computation.4 | convolution fusion | flops 3221749760 | bytes 10485760 | tf_op jit(solution)/shard_map/ski,kij->skj/dot_general | solution.py:51
  543.3 0.9 copy-done.3
  544.2 0.9 copy.71
  545.1 75.8 %reduce-scatter.8.cloned.1.call-done = f32[32,4,512]{2,0,1:T(8,128)} async-done(((f32[512,4,512]{2,0,1:T(8,128)}), f32[32,4,512]{2,0,1:T(8,128)}) %reduce-scatter.8.cloned.1.call-update) | async-done | bytes 262160 | tf_op jit(solution)/shard_map/reduce_scatter | solution.py:50
  620.9 1.8 copy.72
  (82 shorter events, 4.1 us)
Async XLA Ops:
  7.2 528.3 %copy-start = (f32[4,256,512]{2,1,0:T(8,128)S(1)}, f32[4,256,512]{2,1,0:T(8,128)}, u32[]{:S(2)}) copy-start(f32[4,256,512]{2,1,0:T(8,128)} %param.15) | copy-start | bytes 6291460
  7.2 3.3 copy-start.4
  7.2 123.7 %reduce-scatter.4.cloned.1.call-start = ((), (), s32[]{:S(2)}) async-start(), calls=%async_computation.3 | async-start | bytes 4456448 | tf_op jit(solution)/shard_map/reduce_scatter | solution.py:50
  7.2 7.2 %collective-permute-start = (f32[64,1,1024]{2,0,1:T(8,128)}, f32[64,1,1024]{2,0,1:T(8,128)S(1)}, u32[]{:S(2)}, u32[]{:S(2)}) collective-permute-start(f32[64,1,1024]{2,0,1:T(8,128)} %bitcast.59), channel_id=1, source_target_pairs={{0,1},{1,2},{2,3},{3,4},{4,5},{5,6},{6,7},{7,0},{8,9},{9,10},{10,1... | collective-permute-start | bytes 786440 | tf_op jit(solution)/shard_map/ppermute | solution.py:21
  7.3 7.2 %collective-permute-start.1 = (f32[64,1,1024]{2,0,1:T(8,128)}, f32[64,1,1024]{2,0,1:T(8,128)S(1)}, u32[]{:S(2)}, u32[]{:S(2)}) collective-permute-start(f32[64,1,1024]{2,0,1:T(8,128)} %bitcast.60), channel_id=1, source_target_pairs={{0,7},{1,0},{2,1},{3,2},{4,3},{5,4},{6,5},{7,6},{8,15},{9,8},{10,9... | collective-permute-start | bytes 786440 | tf_op jit(solution)/shard_map/ppermute | solution.py:28
  14.5 7.0 %collective-permute-start.2 = (f32[64,1,1024]{2,0,1:T(8,128)S(1)}, f32[64,1,1024]{2,0,1:T(8,128)S(1)}, u32[]{:S(2)}, u32[]{:S(2)}) collective-permute-start(f32[64,1,1024]{2,0,1:T(8,128)S(1)} %collective-permute-done), channel_id=1, source_target_pairs={{0,1},{1,2},{2,3},{3,4},{4,5},{5,6},{6,7},{7,0},{8,9},{9,10},{10,1... | collective-permute-start | bytes 786440 | tf_op jit(solution)/shard_map/ppermute | solution.py:21
  14.5 7.0 %collective-permute-start.3 = (f32[64,1,1024]{2,0,1:T(8,128)S(1)}, f32[64,1,1024]{2,0,1:T(8,128)S(1)}, u32[]{:S(2)}, u32[]{:S(2)}) collective-permute-start(f32[64,1,1024]{2,0,1:T(8,128)S(1)} %collective-permute-done.1), channel_id=1, source_target_pairs={{0,7},{1,0},{2,1},{3,2},{4,3},{5,4},{6,5},{7,6},{8,15},{9,8},{10,9... | collective-permute-start | bytes 786440 | tf_op jit(solution)/shard_map/ppermute | solution.py:28
  21.5 7.0 %collective-permute-start.4 = (f32[64,1,1024]{2,0,1:T(8,128)S(1)}, f32[64,1,1024]{2,0,1:T(8,128)S(1)}, u32[]{:S(2)}, u32[]{:S(2)}) collective-permute-start(f32[64,1,1024]{2,0,1:T(8,128)S(1)} %collective-permute-done.2), channel_id=1, source_target_pairs={{0,1},{1,2},{2,3},{3,4},{4,5},{5,6},{6,7},{7,0},{8,9},{9,10},{10,1... | collective-permute-start | bytes 786440 | tf_op jit(solution)/shard_map/ppermute | solution.py:21
  21.5 7.0 %collective-permute-start.5 = (f32[64,1,1024]{2,0,1:T(8,128)S(1)}, f32[64,1,1024]{2,0,1:T(8,128)S(1)}, u32[]{:S(2)}, u32[]{:S(2)}) collective-permute-start(f32[64,1,1024]{2,0,1:T(8,128)S(1)} %collective-permute-done.3), channel_id=1, source_target_pairs={{0,7},{1,0},{2,1},{3,2},{4,3},{5,4},{6,5},{7,6},{8,15},{9,8},{10,9... | collective-permute-start | bytes 786440 | tf_op jit(solution)/shard_map/ppermute | solution.py:28
  28.5 7.0 %collective-permute-start.6 = (f32[64,1,1024]{2,0,1:T(8,128)S(1)}, f32[64,1,1024]{2,0,1:T(8,128)S(1)}, u32[]{:S(2)}, u32[]{:S(2)}) collective-permute-start(f32[64,1,1024]{2,0,1:T(8,128)S(1)} %collective-permute-done.4), channel_id=1, source_target_pairs={{0,1},{1,2},{2,3},{3,4},{4,5},{5,6},{6,7},{7,0},{8,9},{9,10},{10,1... | collective-permute-start | bytes 786440 | tf_op jit(solution)/shard_map/ppermute | solution.py:21
  52.9 78.1 %copy-start.7 = (s32[4,2]{0,1:T(2,128)S(1)}, s32[4,2]{0,1:T(2,128)}, u32[]{:S(2)}) copy-start(s32[4,2]{0,1:T(2,128)} %param.19) | copy-start | bytes 100
  52.9 78.2 %copy-start.8 = (s32[2,4]{1,0:T(2,128)S(1)}, s32[2,4]{1,0:T(2,128)}, u32[]{:S(2)}) copy-start(s32[2,4]{1,0:T(2,128)} %param.18) | copy-start | bytes 100
  52.9 104.7 %all-gather.5.cloned.1.call-start = ((), (), s32[]{:S(2)}) async-start(), calls=%async_computation.4 | async-start | bytes 2359296 | tf_op jit(solution)/shard_map/all_gather | solution.py:65
  130.9 80.2 %all-gather.7.cloned.1.call-start = ((), (), s32[]{:S(2)}) async-start(), calls=%async_computation.5 | async-start | bytes 2228224 | tf_op jit(solution)/shard_map/all_gather | solution.py:70
  162.2 4.9 copy-start.5
  165.3 119.5 %all-reduce.3.cloned.1.call-start = ((), (), s32[]{:S(2)}) async-start(), calls=%async_computation.6 | async-start | bytes 4194304 | tf_op jit(solution)/shard_map/psum | solution.py:74
  167.9 7.0 %collective-permute-start.7 = (f32[64,2,512]{2,0,1:T(8,128)S(1)}, f32[64,2,512]{2,0,1:T(8,128)S(1)}, u32[]{:S(2)}, u32[]{:S(2)}) collective-permute-start(f32[64,2,512]{2,0,1:T(8,128)S(1)} %get-tuple-element.14), channel_id=1, source_target_pairs={{0,1},{1,2},{2,3},{3,4},{4,5},{5,6},{6,7},{7,0},{8,9},{9,10},{10,1... | collective-permute-start | bytes 786440 | tf_op jit(solution)/shard_map/ppermute | solution.py:21
  168.2 50.1 %collective-permute-start.8 = (f32[64,2,512]{2,0,1:T(8,128)S(1)}, f32[64,2,512]{2,0,1:T(8,128)S(1)}, u32[]{:S(2)}, u32[]{:S(2)}) collective-permute-start(f32[64,2,512]{2,0,1:T(8,128)S(1)} %get-tuple-element.14), channel_id=1, source_target_pairs={{0,7},{1,0},{2,1},{3,2},{4,3},{5,4},{6,5},{7,6},{8,15},{9,8},{10,9... | collective-permute-start | bytes 786440 | tf_op jit(solution)/shard_map/ppermute | solution.py:28
  174.9 44.4 %collective-permute-start.9 = (f32[64,2,512]{2,0,1:T(8,128)S(1)}, f32[64,2,512]{2,0,1:T(8,128)S(1)}, u32[]{:S(2)}, u32[]{:S(2)}) collective-permute-start(f32[64,2,512]{2,0,1:T(8,128)S(1)} %collective-permute-done.7), channel_id=1, source_target_pairs={{0,1},{1,2},{2,3},{3,4},{4,5},{5,6},{6,7},{7,0},{8,9},{9,10},{10,1... | collective-permute-start | bytes 786440 | tf_op jit(solution)/shard_map/ppermute | solution.py:21
  218.2 156.4 %reduce-scatter.6.cloned.1.call-start = ((), (), s32[]{:S(2)}) async-start(), calls=%async_computation.7 | async-start | bytes 4456448 | tf_op jit(solution)/shard_map/reduce_scatter | solution.py:50
  218.2 5.0 collective-permute-start.10
  219.3 7.7 %collective-permute-start.11 = (f32[64,2,512]{2,0,1:T(8,128)S(1)}, f32[64,2,512]{2,0,1:T(8,128)S(1)}, u32[]{:S(2)}, u32[]{:S(2)}) collective-permute-start(f32[64,2,512]{2,0,1:T(8,128)S(1)} %collective-permute-done.9), channel_id=1, source_target_pairs={{0,1},{1,2},{2,3},{3,4},{4,5},{5,6},{6,7},{7,0},{8,9},{9,10},{10,1... | collective-permute-start | bytes 786440 | tf_op jit(solution)/shard_map/ppermute | solution.py:21
  223.2 7.0 %collective-permute-start.12 = (f32[64,2,512]{2,0,1:T(8,128)S(1)}, f32[64,2,512]{2,0,1:T(8,128)S(1)}, u32[]{:S(2)}, u32[]{:S(2)}) collective-permute-start(f32[64,2,512]{2,0,1:T(8,128)S(1)} %collective-permute-done.10), channel_id=1, source_target_pairs={{0,7},{1,0},{2,1},{3,2},{4,3},{5,4},{6,5},{7,6},{8,15},{9,8},{10,9... | collective-permute-start | bytes 786440 | tf_op jit(solution)/shard_map/ppermute | solution.py:28
  227.0 7.9 %collective-permute-start.13 = (f32[64,2,512]{2,0,1:T(8,128)S(1)}, f32[64,2,512]{2,0,1:T(8,128)S(1)}, u32[]{:S(2)}, u32[]{:S(2)}) collective-permute-start(f32[64,2,512]{2,0,1:T(8,128)S(1)} %collective-permute-done.11), channel_id=1, source_target_pairs={{0,1},{1,2},{2,3},{3,4},{4,5},{5,6},{6,7},{7,0},{8,9},{9,10},{10,1... | collective-permute-start | bytes 786440 | tf_op jit(solution)/shard_map/ppermute | solution.py:21
  297.0 103.4 %all-gather.9.cloned.1.call-start = ((), (), s32[]{:S(2)}) async-start(), calls=%async_computation.8 | async-start | bytes 2359296 | tf_op jit(solution)/shard_map/all_gather | solution.py:65
  374.6 89.3 %all-gather.11.cloned.1.call-start = ((), (), s32[]{:S(2)}) async-start(), calls=%async_computation.9 | async-start | bytes 2228224 | tf_op jit(solution)/shard_map/all_gather | solution.py:70
  409.0 3.0 copy-start.1
  414.4 49.5 %copy-start.2 = (f32[4,256,256]{2,1,0:T(8,128)S(1)}, f32[4,256,256]{2,1,0:T(8,128)}, u32[]{:S(2)}) copy-start(f32[4,256,256]{2,1,0:T(8,128)} %param.17) | copy-start | bytes 3145732
  417.4 2.4 copy-start.6
  418.1 117.3 %all-reduce.5.cloned.1.call-start = ((), (), s32[]{:S(2)}) async-start(), calls=%async_computation.10 | async-start | bytes 4194304 | tf_op jit(solution)/shard_map/psum | solution.py:74
  420.6 7.3 %collective-permute-start.14 = (f32[64,4,256]{2,0,1:T(8,128)}, f32[64,4,256]{2,0,1:T(8,128)}, u32[]{:S(2)}, u32[]{:S(2)}) collective-permute-start(f32[64,4,256]{2,0,1:T(8,128)} %get-tuple-element.12), channel_id=1, source_target_pairs={{0,1},{1,2},{2,3},{3,4},{4,5},{5,6},{6,7},{7,0},{8,9},{9,10},{10,1... | collective-permute-start | bytes 786440 | tf_op jit(solution)/shard_map/ppermute | solution.py:21
  420.9 48.0 %collective-permute-start.15 = (f32[64,4,256]{2,0,1:T(8,128)}, f32[64,4,256]{2,0,1:T(8,128)}, u32[]{:S(2)}, u32[]{:S(2)}) collective-permute-start(f32[64,4,256]{2,0,1:T(8,128)} %get-tuple-element.12), channel_id=1, source_target_pairs={{0,7},{1,0},{2,1},{3,2},{4,3},{5,4},{6,5},{7,6},{8,15},{9,8},{10,9... | collective-permute-start | bytes 786440 | tf_op jit(solution)/shard_map/ppermute | solution.py:28
  427.9 42.1 %collective-permute-start.16 = (f32[64,4,256]{2,0,1:T(8,128)}, f32[64,4,256]{2,0,1:T(8,128)S(1)}, u32[]{:S(2)}, u32[]{:S(2)}) collective-permute-start(f32[64,4,256]{2,0,1:T(8,128)} %collective-permute-done.14), channel_id=1, source_target_pairs={{0,1},{1,2},{2,3},{3,4},{4,5},{5,6},{6,7},{7,0},{8,9},{9,10},{10,1... | collective-permute-start | bytes 786440 | tf_op jit(solution)/shard_map/ppermute | solution.py:21
  468.8 152.1 %reduce-scatter.8.cloned.1.call-start = ((), (), s32[]{:S(2)}) async-start(), calls=%async_computation.11 | async-start | bytes 4456448 | tf_op jit(solution)/shard_map/reduce_scatter | solution.py:50
  468.9 5.3 collective-permute-start.17
  470.0 8.0 %collective-permute-start.18 = (f32[64,4,256]{2,0,1:T(8,128)S(1)}, f32[64,4,256]{2,0,1:T(8,128)S(1)}, u32[]{:S(2)}, u32[]{:S(2)}) collective-permute-start(f32[64,4,256]{2,0,1:T(8,128)S(1)} %collective-permute-done.16), channel_id=1, source_target_pairs={{0,1},{1,2},{2,3},{3,4},{4,5},{5,6},{6,7},{7,0},{8,9},{9,10},{10,1... | collective-permute-start | bytes 786440 | tf_op jit(solution)/shard_map/ppermute | solution.py:21
  474.2 6.9 %collective-permute-start.19 = (f32[64,4,256]{2,0,1:T(8,128)S(1)}, f32[64,4,256]{2,0,1:T(8,128)S(1)}, u32[]{:S(2)}, u32[]{:S(2)}) collective-permute-start(f32[64,4,256]{2,0,1:T(8,128)S(1)} %collective-permute-done.17), channel_id=1, source_target_pairs={{0,7},{1,0},{2,1},{3,2},{4,3},{5,4},{6,5},{7,6},{8,15},{9,8},{10,9... | collective-permute-start | bytes 786440 | tf_op jit(solution)/shard_map/ppermute | solution.py:28
  477.9 7.7 %collective-permute-start.20 = (f32[64,4,256]{2,0,1:T(8,128)S(1)}, f32[64,4,256]{2,0,1:T(8,128)S(1)}, u32[]{:S(2)}, u32[]{:S(2)}) collective-permute-start(f32[64,4,256]{2,0,1:T(8,128)S(1)} %collective-permute-done.18), channel_id=1, source_target_pairs={{0,1},{1,2},{2,3},{3,4},{4,5},{5,6},{6,7},{7,0},{8,9},{9,10},{10,1... | collective-permute-start | bytes 786440 | tf_op jit(solution)/shard_map/ppermute | solution.py:21
  543.2 0.9 copy-start.3
Sparse Core Ops, SparseCore 0:
  53.0 77.7 reduce-scatter.3
  133.2 24.3 all-gather.4
  165.4 45.5 all-gather.6
  218.3 66.4 all-reduce.2
  297.1 77.3 reduce-scatter.5
  376.1 24.3 all-gather.8
  418.2 45.5 all-gather.10
  469.0 66.4 all-reduce.4
  543.4 77.4 reduce-scatter.7
